TPU v7x, 256 devices: a whole 4x4x8 slice. The times are simulated.
256 devices in a mesh: pair: 128 (over x, z, y), aux: 2 (over core).
Axes of the slice: x: 4, y: 4, z: 8, core: 2. Of those that a mesh axis runs over, the one named last changes fastest.
Arguments:
- amplitudes: bfloat16 [16384, 128, 128], P('pair', 'aux'), may hold values from -6 to 6
- k_term: bfloat16 [16384, 128, 128], P('pair', 'aux'), may hold values from -6 to 6
- margin_table: bfloat16 [1024, 128, 128], P('pair'), may hold values from -0.5 to 0.5
- margin_index: int32 [16384], P('pair'), may hold values from 0 to 7
- factors: bfloat16 [128, 512, 128], P('pair', 'aux'), may hold values from -6 to 6
- vir_energy: float32 [16384, 128], P('pair'), may hold values from 0.5 to 3
- occ_energy: float32 [128], replicated, may hold values from -2 to -0.3
- pair_owner: int32 [16384, 1], P('pair'), may hold values from 0 to 127; in each aligned block of 128 rows (0 to 127, 128 to 255, ...) at most 2 rows name the same one
Outputs:
- updated: bfloat16 [16384, 128, 128], P('pair', 'aux')
Inputs may be any that keep to these rules, and one draw needn't show every extreme that they name: `pair_owner`: no more than 2 of the 128 pairs of one aligned block name the same owner. `margin_index`: an index into the 8 margin blocks that belong to the pair's aligned block of 128 pairs.
All inputs are finite; a program needn't handle non-finite values.
Results may differ from a plain program's by a relative error of at most 0.0055.
Values may be sent and summed in bfloat16 or wider, within the bound.
No kernel may reach another device: no remote copies, remote signals or barrier semaphores. Data moves between devices by JAX's collectives and lax.ppermute only.
A program may use at most 128 MiB of HBM per device.

v0:
```python
import jax
import jax.numpy as jnp
from jax import lax
from jax.sharding import PartitionSpec as P

RING_ORDER = ((8, 4), (4, 1), (4, 32))


def ring_gather(block, size, stride, total):
    pieces = [block]
    for shift in range(1, size):
        perm = []
        for device in range(total):
            coord = device // stride % size
            perm.append((device, device + ((coord + shift) % size - coord) * stride))
        pieces.append(lax.ppermute(block, "pair", perm))
    return jnp.stack(pieces)


def local(
    amplitudes, k_term, margin_table, margin_index, factors, vir_energy, occ_energy, pair_owner
):
    axis_pairs = lax.axis_size("pair")
    aux_count = lax.axis_size("aux")
    own_index = lax.axis_index("pair")
    aux_index = lax.axis_index("aux")
    pair_count = amplitudes.shape[0]
    row_count = amplitudes.shape[1]
    vir_width = amplitudes.shape[2]
    aux_rows = factors.shape[1]
    ovl_count = margin_table.shape[0]
    cycle_scale = float(vir_width * aux_rows * aux_count * pair_count) ** (-0.5)
    every_factor = lax.all_gather(factors[0], ("pair", "aux"), axis=0, tiled=True)
    every_factor = every_factor.reshape(axis_pairs, aux_count * aux_rows, vir_width)
    own_factors = lax.dynamic_index_in_dim(every_factor, own_index, 0, keepdims=False)
    other_amp = lax.ppermute(amplitudes, "aux", perm=[(0, 1), (1, 0)])
    full_amp = jnp.where(
        aux_index == 0,
        jnp.concatenate([amplitudes, other_amp], axis=1),
        jnp.concatenate([other_amp, amplitudes], axis=1),
    )
    block_pick = (margin_index[:, None] == jnp.arange(ovl_count, dtype=jnp.int32)[None, :]).astype(
        jnp.bfloat16
    )
    margin = jnp.einsum(
        "po,oab->pab", block_pick, margin_table, preferred_element_type=jnp.float32
    ).astype(jnp.bfloat16)
    halfway = jnp.einsum(
        "pca,pab->pcb", full_amp, margin, preferred_element_type=jnp.float32
    ).astype(jnp.bfloat16)
    rotated = jnp.einsum(
        "pac,pab->pcb", margin, halfway, preferred_element_type=jnp.float32
    ).astype(jnp.bfloat16)
    rotated = lax.dynamic_slice_in_dim(rotated, aux_index * row_count, row_count, 1)
    pair_dest = pair_owner[:, 0]
    owner_pick = (jnp.arange(axis_pairs, dtype=jnp.int32)[:, None] == pair_dest[None, :]).astype(
        jnp.bfloat16
    )
    outgoing = jnp.einsum(
        "jp,pcb->jcb", owner_pick, rotated, preferred_element_type=jnp.float32
    ).astype(jnp.bfloat16)
    occ_sum = occ_energy[own_index] + occ_energy[pair_dest]
    energy_rows = lax.dynamic_slice_in_dim(vir_energy, aux_index * row_count, row_count, 1)
    denominator = energy_rows[:, :, None] + vir_energy[:, None, :] - occ_sum[:, None, None]
    inverse = 1.0 / denominator
    prior = amplitudes.astype(jnp.float32) - k_term.astype(jnp.float32) * inverse
    outgoing, prior, inverse = lax.optimization_barrier((outgoing, prior, inverse))
    incoming = lax.all_to_all(outgoing, "pair", 0, 0, tiled=True)
    dressed = jnp.einsum(
        "ica,iqa->cq", incoming, every_factor, preferred_element_type=jnp.float32
    ).astype(jnp.bfloat16)
    local_cycle = jnp.dot(dressed, own_factors, preferred_element_type=jnp.float32)
    cycle_vals = (cycle_scale * local_cycle).astype(jnp.bfloat16)
    returned = cycle_vals
    ring_offset = jnp.zeros_like(pair_dest)
    ring_scale = 1
    for size, stride in RING_ORDER:
        returned = ring_gather(returned, size, stride, axis_pairs)
        own_coord = own_index // stride % size
        dest_coord = pair_dest // stride % size
        ring_offset = ring_offset + (own_coord - dest_coord) % size * ring_scale
        ring_scale = ring_scale * size
    returned = returned.reshape(axis_pairs, row_count, vir_width)
    offset_pick = (jnp.arange(axis_pairs, dtype=jnp.int32)[:, None] == ring_offset[None, :]).astype(
        jnp.bfloat16
    )
    own_cycle = jnp.einsum(
        "jp,jca->pca", offset_pick, returned, preferred_element_type=jnp.float32
    ).astype(jnp.bfloat16)
    cycle_term = jnp.einsum("pca,pba->pcb", own_cycle, margin, preferred_element_type=jnp.float32)
    updated = prior - cycle_term * inverse
    return updated.astype(jnp.bfloat16)


def solution(mesh):
    placed = (
        P("pair", "aux", None),
        P("pair", "aux", None),
        P("pair", None, None),
        P("pair"),
        P("pair", "aux", None),
        P("pair", None),
        P(),
        P("pair", None),
    )
    return jax.shard_map(
        local, mesh=mesh, in_specs=placed, out_specs=P("pair", "aux", None), check_vma=False
    )
```

profile of v0, /device:TPU:3, one launch (start us, length us, event | category | flops | bytes accessed | tf_op | source)
XLA Modules:
  0.0 224.5 jit_solution(11171059530084323425)
XLA Ops:
  8.0 1.2 dynamic_slice.15
  9.9 1.6 gather_fusion
  11.5 1.1 constant_dynamic-slice_fusion
  13.3 3.9 %convolution_convert_fusion = bf16[128,128,128]{2,0,1:T(8,128)(2,1)} fusion(bf16[8,128,128]{2,1,0:T(8,128)(2,1)S(1)} %copy-done, s32[128]{0:T(128)} %param.11), kind=kOutput, calls=%fused_computation.19 | convolution fusion | flops 35652608 | bytes 4456960 | tf_op jit(solution)/shard_map/po,oab->pab/dot_general | solution.py:45
  17.2 4.8 %subtract_divide_fusion = (f32[128,64,128]{2,1,0:T(8,128)}, f32[128,64,128]{2,1,0:T(8,128)}) fusion(f32[128]{0:T(128)S(1)} %broadcast_add_fusion, f32[128,128]{1,0:T(8,128)S(1)} %copy-done.5, f32[128,64]{1,0:T(8,128)S(1)} %constant_dynamic-slice_fusion, bf16[128,64,128]{2,1,0:T(8,128)(2,1)S(1)} %copy-done.3, bf16[128,64,128]{2,1,0:T(8,128)(2,1)S(1)} %copy-done.4), kind=kLoop, calls=%fused_computation.11 | loop fusion | flops 7340032 | bytes 12681728 | tf_op jit(solution)/shard_map/div | solution.py:65
  22.0 14.9 %fusion.6 = bf16[128,128,128]{2,1,0:T(8,128)(2,1)} fusion(bf16[128,128,128]{2,0,1:T(8,128)(2,1)} %convolution_convert_fusion, bf16[128,64,128]{2,1,0:T(8,128)(2,1)} %collective-permute-done, bf16[128,64,128]{2,1,0:T(8,128)(2,1)} %param.8, pred[]{:T(512)S(6)} %eq.62), kind=kOutput, calls=%fused_computation.12 | convolution fusion | flops 1094713344 | bytes 12582913 | tf_op jit(solution)/shard_map/pac,pab->pcb/dot_general | solution.py:51
  36.9 1.8 dynamic-slice_convert_fusion
  38.7 1.8 fusion.22
  40.4 1.4 copy.17
  41.8 70.9 %all_to_all.5 = bf16[128,64,128]{2,1,0:T(8,128)(2,1)S(1)} all-to-all(bf16[128,64,128]{2,1,0:T(8,128)(2,1)S(1)} %copy.17), channel_id=1, replica_groups=mesh['pair'=128,'aux'=2] {'pair'}, dimensions={0} | all-to-all | bytes 4194304 | tf_op jit(solution)/shard_map/all_to_all | solution.py:68
  112.7 32.9 %all-gather.3.cloned.1.call-done = bf16[1,65536,128]{2,1,0:T(8,128)(2,1)} async-done(((bf16[1,256,128]{2,1,0:T(8,128)(2,1)}), bf16[1,65536,128]{2,1,0:T(8,128)(2,1)}) %all-gather.3.cloned.1.call-update) | async-done | bytes 16777232 | tf_op jit(solution)/shard_map/all_gather | solution.py:33
  145.6 11.0 %constant_dynamic-update-slice_fusion.7 = (bf16[8,64,128]{2,1,0:T(8,128)(2,1)S(1)}, bf16[64,128]{1,0:T(8,128)(2,1)S(1)}) fusion(bf16[128,512,128]{2,1,0:T(8,128)(2,1)} %bitcast.56, s32[]{:T(128)S(6)} %select_n.115, bf16[128,64,128]{2,1,0:T(8,128)(2,1)S(1)} %all_to_all.5), kind=kOutput, calls=%fused_computation.49 | convolution fusion | flops 1082179584 | bytes 19038212 | tf_op jit(solution)/shard_map/dot_general | solution.py:72
  157.1 1.9 collective-permute-start.2
  159.0 1.9 collective-permute-start.3
  160.8 2.7 %collective-permute-start.4 = (bf16[64,128]{1,0:T(8,128)(2,1)S(1)}, bf16[64,128]{1,0:T(8,128)(2,1)S(1)}, u32[]{:S(2)}, u32[]{:S(2)}) collective-permute-start(bf16[64,128]{1,0:T(8,128)(2,1)S(1)} %get-tuple-element.16), channel_id=1, source_target_pairs={{0,32},{2,34},{4,36},{6,38},{8,40},{10,42},{12,44},{14,46},{16,48}... | collective-permute-start | bytes 49160 | tf_op jit(solution)/shard_map/ppermute | solution.py:16
  163.5 2.3 %collective-permute-start.5 = (bf16[64,128]{1,0:T(8,128)(2,1)S(1)}, bf16[64,128]{1,0:T(8,128)(2,1)S(1)}, u32[]{:S(2)}, u32[]{:S(2)}) collective-permute-start(bf16[64,128]{1,0:T(8,128)(2,1)S(1)} %get-tuple-element.16), channel_id=1, source_target_pairs={{0,40},{2,42},{4,44},{6,46},{8,48},{10,50},{12,52},{14,54},{16,56}... | collective-permute-start | bytes 49160 | tf_op jit(solution)/shard_map/ppermute | solution.py:16
  165.8 2.1 collective-permute-start.6
  168.0 0.8 collective-permute-start.7
  168.8 0.8 collective-permute-done.6
  169.6 1.0 collective-permute-done.7
  170.8 2.2 collective-permute-start.9
  173.0 1.2 collective-permute-start.10
  174.2 2.8 %collective-permute-done.8 = bf16[8,64,128]{2,1,0:T(8,128)(2,1)S(1)} collective-permute-done((bf16[8,64,128]{2,1,0:T(8,128)(2,1)S(1)}, bf16[8,64,128]{2,1,0:T(8,128)(2,1)S(1)}, u32[]{:S(2)}, u32[]{:S(2)}) %collective-permute-start.8) | collective-permute-done | bytes 131104 | tf_op jit(solution)/shard_map/ppermute | solution.py:16
  177.7 1.3 collective-permute-start.11
  179.0 1.7 collective-permute-start.12
  180.7 1.1 collective-permute-start.13
  181.8 5.0 %collective-permute-done.11 = bf16[4,8,64,128]{3,2,1,0:T(8,128)(2,1)S(1)} collective-permute-done((bf16[4,8,64,128]{3,2,1,0:T(8,128)(2,1)S(1)}, bf16[4,8,64,128]{3,2,1,0:T(8,128)(2,1)S(1)}, u32[]{:S(2)}, u32[]{:S(2)}) %collective-permute-start.11) | collective-permute-done | bytes 524320 | tf_op jit(solution)/shard_map/ppermute | solution.py:16
  186.8 3.0 %collective-permute-done.12 = bf16[4,8,64,128]{3,2,1,0:T(8,128)(2,1)S(1)} collective-permute-done((bf16[4,8,64,128]{3,2,1,0:T(8,128)(2,1)S(1)}, bf16[4,8,64,128]{3,2,1,0:T(8,128)(2,1)S(1)}, u32[]{:S(2)}, u32[]{:S(2)}) %collective-permute-start.12) | collective-permute-done | bytes 524320 | tf_op jit(solution)/shard_map/ppermute | solution.py:16
  189.8 15.8 %collective-permute-done.13 = bf16[4,8,64,128]{3,2,1,0:T(8,128)(2,1)S(1)} collective-permute-done((bf16[4,8,64,128]{3,2,1,0:T(8,128)(2,1)S(1)}, bf16[4,8,64,128]{3,2,1,0:T(8,128)(2,1)S(1)}, u32[]{:S(2)}, u32[]{:S(2)}) %collective-permute-start.13) | collective-permute-done | bytes 524320 | tf_op jit(solution)/shard_map/ppermute | solution.py:16
  205.9 1.7 fusion.25
  207.8 1.3 copy-done.2
  209.1 8.6 %subtract_convert_fusion = bf16[128,64,128]{2,1,0:T(8,128)(2,1)} fusion(f32[128,64,128]{2,1,0:T(8,128)} %get-tuple-element.8, f32[128,64,128]{2,1,0:T(8,128)S(1)} %copy-done.2, bf16[128,128,128]{2,0,1:T(8,128)(2,1)S(1)} %copy-done.1, bf16[128,64,128]{2,0,1:T(8,128)(2,1)S(1)} %fusion.25), kind=kOutput, calls=%fused_computation.9 | convolution fusion | flops 271581184 | bytes 16777216 | tf_op jit(solution)/shard_map/pca,pba->pcb/dot_general | solution.py:90
  (39 shorter events, 4.6 us)
Async XLA Ops:
  6.5 6.7 %copy-start = (bf16[8,128,128]{2,1,0:T(8,128)(2,1)S(1)}, bf16[8,128,128]{2,1,0:T(8,128)(2,1)}, u32[]{:S(2)}) copy-start(bf16[8,128,128]{2,1,0:T(8,128)(2,1)} %param.10) | copy-start | bytes 786436
  6.5 10.7 %copy-start.5 = (f32[128,128]{1,0:T(8,128)S(1)}, f32[128,128]{1,0:T(8,128)}, u32[]{:S(2)}) copy-start(f32[128,128]{1,0:T(8,128)} %param.13) | copy-start | bytes 196612
  6.5 10.7 %copy-start.3 = (bf16[128,64,128]{2,1,0:T(8,128)(2,1)S(1)}, bf16[128,64,128]{2,1,0:T(8,128)(2,1)}, u32[]{:S(2)}) copy-start(bf16[128,64,128]{2,1,0:T(8,128)(2,1)} %param.9) | copy-start | bytes 6291460
  6.5 139.0 %all-gather.3.cloned.1.call-start = ((), (), s32[]{:S(2)}) async-start(), calls=%async_computation.1 | async-start | bytes 16842752 | tf_op jit(solution)/shard_map/all_gather | solution.py:33
  7.3 14.7 %collective-permute-start = (bf16[128,64,128]{2,1,0:T(8,128)(2,1)}, bf16[128,64,128]{2,1,0:T(8,128)(2,1)}, u32[]{:S(2)}, u32[]{:S(2)}) collective-permute-start(bf16[128,64,128]{2,1,0:T(8,128)(2,1)} %param.8), channel_id=1, source_target_pairs={{0,1},{1,0},{2,3},{3,2},{4,5},{5,4},{6,7},{7,6},{8,9},{9,8},{10,11... | collective-permute-start | bytes 6291464 | tf_op jit(solution)/shard_map/ppermute | solution.py:36
  11.5 5.7 %copy-start.4 = (bf16[128,64,128]{2,1,0:T(8,128)(2,1)S(1)}, bf16[128,64,128]{2,1,0:T(8,128)(2,1)}, u32[]{:S(2)}) copy-start(bf16[128,64,128]{2,1,0:T(8,128)(2,1)} %param.8) | copy-start | bytes 6291460
  36.9 1.8 copy-start.6
  156.6 9.2 %collective-permute-start.1 = (bf16[64,128]{1,0:T(8,128)(2,1)S(1)}, bf16[64,128]{1,0:T(8,128)(2,1)S(1)}, u32[]{:S(2)}, u32[]{:S(2)}) collective-permute-start(bf16[64,128]{1,0:T(8,128)(2,1)S(1)} %get-tuple-element.16), channel_id=1, source_target_pairs={{0,8},{2,10},{4,12},{6,14},{8,16},{10,18},{12,20},{14,22},{16,24},... | collective-permute-start | bytes 49160 | tf_op jit(solution)/shard_map/ppermute | solution.py:16
  157.1 10.9 %collective-permute-start.2 = (bf16[64,128]{1,0:T(8,128)(2,1)S(1)}, bf16[64,128]{1,0:T(8,128)(2,1)S(1)}, u32[]{:S(2)}, u32[]{:S(2)}) collective-permute-start(bf16[64,128]{1,0:T(8,128)(2,1)S(1)} %get-tuple-element.16), channel_id=1, source_target_pairs={{0,16},{2,18},{4,20},{6,22},{8,24},{10,26},{12,28},{14,30},{16,32}... | collective-permute-start | bytes 49160 | tf_op jit(solution)/shard_map/ppermute | solution.py:16
  159.0 9.8 %collective-permute-start.3 = (bf16[64,128]{1,0:T(8,128)(2,1)S(1)}, bf16[64,128]{1,0:T(8,128)(2,1)S(1)}, u32[]{:S(2)}, u32[]{:S(2)}) collective-permute-start(bf16[64,128]{1,0:T(8,128)(2,1)S(1)} %get-tuple-element.16), channel_id=1, source_target_pairs={{0,24},{2,26},{4,28},{6,30},{8,32},{10,34},{12,36},{14,38},{16,40}... | collective-permute-start | bytes 49160 | tf_op jit(solution)/shard_map/ppermute | solution.py:16
  160.8 8.0 %collective-permute-start.4 = (bf16[64,128]{1,0:T(8,128)(2,1)S(1)}, bf16[64,128]{1,0:T(8,128)(2,1)S(1)}, u32[]{:S(2)}, u32[]{:S(2)}) collective-permute-start(bf16[64,128]{1,0:T(8,128)(2,1)S(1)} %get-tuple-element.16), channel_id=1, source_target_pairs={{0,32},{2,34},{4,36},{6,38},{8,40},{10,42},{12,44},{14,46},{16,48}... | collective-permute-start | bytes 49160 | tf_op jit(solution)/shard_map/ppermute | solution.py:16
  163.5 5.3 %collective-permute-start.5 = (bf16[64,128]{1,0:T(8,128)(2,1)S(1)}, bf16[64,128]{1,0:T(8,128)(2,1)S(1)}, u32[]{:S(2)}, u32[]{:S(2)}) collective-permute-start(bf16[64,128]{1,0:T(8,128)(2,1)S(1)} %get-tuple-element.16), channel_id=1, source_target_pairs={{0,40},{2,42},{4,44},{6,46},{8,48},{10,50},{12,52},{14,54},{16,56}... | collective-permute-start | bytes 49160 | tf_op jit(solution)/shard_map/ppermute | solution.py:16
  165.8 3.8 %collective-permute-start.6 = (bf16[64,128]{1,0:T(8,128)(2,1)S(1)}, bf16[64,128]{1,0:T(8,128)(2,1)S(1)}, u32[]{:S(2)}, u32[]{:S(2)}) collective-permute-start(bf16[64,128]{1,0:T(8,128)(2,1)S(1)} %get-tuple-element.16), channel_id=1, source_target_pairs={{0,48},{2,50},{4,52},{6,54},{8,56},{10,58},{12,60},{14,62},{16,0},... | collective-permute-start | bytes 49160 | tf_op jit(solution)/shard_map/ppermute | solution.py:16
  168.0 2.7 %collective-permute-start.7 = (bf16[64,128]{1,0:T(8,128)(2,1)S(1)}, bf16[64,128]{1,0:T(8,128)(2,1)S(1)}, u32[]{:S(2)}, u32[]{:S(2)}) collective-permute-start(bf16[64,128]{1,0:T(8,128)(2,1)S(1)} %get-tuple-element.16), channel_id=1, source_target_pairs={{0,56},{2,58},{4,60},{6,62},{8,0},{10,2},{12,4},{14,6},{16,8},{18,... | collective-permute-start | bytes 49160 | tf_op jit(solution)/shard_map/ppermute | solution.py:16
  170.6 6.4 %collective-permute-start.8 = (bf16[8,64,128]{2,1,0:T(8,128)(2,1)S(1)}, bf16[8,64,128]{2,1,0:T(8,128)(2,1)S(1)}, u32[]{:S(2)}, u32[]{:S(2)}) collective-permute-start(bf16[8,64,128]{2,1,0:T(8,128)(2,1)S(1)} %constant_dynamic-update-slice_fusion), channel_id=1, source_target_pairs={{0,2},{2,4},{4,6},{6,0},{8,10},{10,12},{12,14},{14,8},{16,18},{18,... | collective-permute-start | bytes 393224 | tf_op jit(solution)/shard_map/ppermute | solution.py:16
  170.8 6.3 %collective-permute-start.9 = (bf16[8,64,128]{2,1,0:T(8,128)(2,1)S(1)}, bf16[8,64,128]{2,1,0:T(8,128)(2,1)S(1)}, u32[]{:S(2)}, u32[]{:S(2)}) collective-permute-start(bf16[8,64,128]{2,1,0:T(8,128)(2,1)S(1)} %constant_dynamic-update-slice_fusion), channel_id=1, source_target_pairs={{0,4},{2,6},{4,0},{6,2},{8,12},{10,14},{12,8},{14,10},{16,20},{18,... | collective-permute-start | bytes 393224 | tf_op jit(solution)/shard_map/ppermute | solution.py:16
  173.0 4.6 %collective-permute-start.10 = (bf16[8,64,128]{2,1,0:T(8,128)(2,1)S(1)}, bf16[8,64,128]{2,1,0:T(8,128)(2,1)S(1)}, u32[]{:S(2)}, u32[]{:S(2)}) collective-permute-start(bf16[8,64,128]{2,1,0:T(8,128)(2,1)S(1)} %constant_dynamic-update-slice_fusion), channel_id=1, source_target_pairs={{0,6},{2,0},{4,2},{6,4},{8,14},{10,8},{12,10},{14,12},{16,22},{18,... | collective-permute-start | bytes 393224 | tf_op jit(solution)/shard_map/ppermute | solution.py:16
  177.7 9.1 %collective-permute-start.11 = (bf16[4,8,64,128]{3,2,1,0:T(8,128)(2,1)S(1)}, bf16[4,8,64,128]{3,2,1,0:T(8,128)(2,1)S(1)}, u32[]{:S(2)}, u32[]{:S(2)}) collective-permute-start(bf16[4,8,64,128]{3,2,1,0:T(8,128)(2,1)S(1)} %get-tuple-element.12), channel_id=1, source_target_pairs={{0,64},{2,66},{4,68},{6,70},{8,72},{10,74},{12,76},{14,78},{16,80}... | collective-permute-start | bytes 1572872 | tf_op jit(solution)/shard_map/ppermute | solution.py:16
  179.0 10.8 %collective-permute-start.12 = (bf16[4,8,64,128]{3,2,1,0:T(8,128)(2,1)S(1)}, bf16[4,8,64,128]{3,2,1,0:T(8,128)(2,1)S(1)}, u32[]{:S(2)}, u32[]{:S(2)}) collective-permute-start(bf16[4,8,64,128]{3,2,1,0:T(8,128)(2,1)S(1)} %get-tuple-element.12), channel_id=1, source_target_pairs={{0,128},{2,130},{4,132},{6,134},{8,136},{10,138},{12,140},{14,142}... | collective-permute-start | bytes 1572872 | tf_op jit(solution)/shard_map/ppermute | solution.py:16
  180.7 24.9 %collective-permute-start.13 = (bf16[4,8,64,128]{3,2,1,0:T(8,128)(2,1)S(1)}, bf16[4,8,64,128]{3,2,1,0:T(8,128)(2,1)S(1)}, u32[]{:S(2)}, u32[]{:S(2)}) collective-permute-start(bf16[4,8,64,128]{3,2,1,0:T(8,128)(2,1)S(1)} %get-tuple-element.12), channel_id=1, source_target_pairs={{0,192},{2,194},{4,196},{6,198},{8,200},{10,202},{12,204},{14,206}... | collective-permute-start | bytes 1572872 | tf_op jit(solution)/shard_map/ppermute | solution.py:16
  205.6 2.2 copy-start.1
  205.6 3.5 %copy-start.2 = (f32[128,64,128]{2,1,0:T(8,128)S(1)}, f32[128,64,128]{2,1,0:T(8,128)}, u32[]{:S(2)}) copy-start(f32[128,64,128]{2,1,0:T(8,128)} %get-tuple-element.10) | copy-start | bytes 12582916
Sparse Core Ops, SparseCore 0:
  11.0 134.4 all-gather.2
where the time goes:
time: 225 us
  blocking collectives  70.9 us (32%)
  waiting for transfers between devices  62.6 us (28%)
  matrix products  42 us (19%)
  starting transfers between devices  20.6 us (9%)
  between operations  13.5 us (6%)
  local copies, waits for them, and re-layouts  8.56 us (4%)
  other arithmetic  6.47 us (3%)
    all_to_all x1, blocking collectives, local(): incoming = lax.all_to_all(outgoing, 'pair', 0, 0, tiled=True)  70.9 us
    all_gather x1, waiting for transfers between devices, local(): lax.all_gather(factors[0], ('pair', 'aux'), axis=0, tiled=True)  32.9 us
    ppermute x13, waiting for transfers between devices, ring_gather(): pieces.append(lax.ppermute(block, 'pair', perm))  29 us
    ppermute x13, starting transfers between devices, ring_gather(): pieces.append(lax.ppermute(block, 'pair', perm))  19.8 us
    dot_general x1, matrix products, local(): jnp.einsum('pac,pab->pcb', margin, halfway, preferred_element_type=jnp.fl...  14.9 us
    dot_general x1, matrix products, local(): jnp.dot(dressed, own_factors, preferred_element_type=jnp.float32)  11 us
    dot_general x1, matrix products, local(): jnp.einsum('pca,pba->pcb', own_cycle, margin, preferred_element_type=jnp....  8.63 us
    div x1, other arithmetic, local(): inverse = 1.0 / denominator  4.77 us
  transfers between devices with their start and end apart: 15, of which 8 were waited for; matrix products, arithmetic and copies ran while one was open for 15% of the time, Pallas kernels for 0%

commit v1 on v0

--- a/solution.py
+++ b/solution.py
@@ -1,9 +1,20 @@
+import functools
 import jax
 import jax.numpy as jnp
 from jax import lax
 from jax.sharding import PartitionSpec as P
 
 RING_ORDER = ((8, 4), (4, 1), (4, 32))
+
+
+def feed_islands(panel, array_dim):
+    parts_out = jax.lax.axis_size(("pair", "aux"))
+    state_now = jnp.stack([panel] * parts_out)
+    g_now = jax.lax.all_to_all(state_now, concat_axis=0, split_axis=0, axis_name=("pair", "aux"))
+    return jnp.concatenate(g_now, axis=array_dim)
+
+
+map_masks = functools.partial(feed_islands, array_dim=0)
 
 
 def ring_gather(block, size, stride, total):
@@ -30,7 +41,7 @@
     aux_rows = factors.shape[1]
     ovl_count = margin_table.shape[0]
     cycle_scale = float(vir_width * aux_rows * aux_count * pair_count) ** (-0.5)
-    every_factor = lax.all_gather(factors[0], ("pair", "aux"), axis=0, tiled=True)
+    every_factor = map_masks(factors[0])
     every_factor = every_factor.reshape(axis_pairs, aux_count * aux_rows, vir_width)
     own_factors = lax.dynamic_index_in_dim(every_factor, own_index, 0, keepdims=False)
     other_amp = lax.ppermute(amplitudes, "aux", perm=[(0, 1), (1, 0)])

time: 225 us -> 555 us (2.47)
  blocking collectives: 70.9 us -> 440 us
  waiting for transfers between devices: 62.6 us -> 34.1 us
  between operations: 13.5 us -> 0.15 us
    all_to_all x0 -> x1, blocking collectives: none -> 376 us  [feed_islands(): jax.lax.all_to_all(state_now, concat_axis=0, split_axis=0, axis_name=('pa...]
    all_gather x1 -> x0, waiting for transfers between devices: 32.9 us -> none  [local(): lax.all_gather(factors[0], ('pair', 'aux'), axis=0, tiled=True)]
    all_to_all x1, blocking collectives: 70.9 us -> 64.2 us  [local(): incoming = lax.all_to_all(outgoing, 'pair', 0, 0, tiled=True)]
  transfers between devices with their start and end apart: 15 -> 14, of which waited for: 8 -> 8; matrix products, arithmetic and copies ran while one was open for 15% -> 3% of each run, Pallas kernels for 0% -> 0%
where the time goes in v1:
time: 555 us; the launch traced here: 553 us
  blocking collectives  440 us (79%)
  matrix products  42.1 us (8%)
  waiting for transfers between devices  34.1 us (6%)
  starting transfers between devices  17.1 us (3%)
  local copies, waits for them, and re-layouts  12.8 us (2%)
  other arithmetic  6.48 us (1%)
    all_to_all x1, blocking collectives, feed_islands(): jax.lax.all_to_all(state_now, concat_axis=0, split_axis=0, axis_name=('pa...  376 us
    all_to_all x1, blocking collectives, local(): incoming = lax.all_to_all(outgoing, 'pair', 0, 0, tiled=True)  64.2 us
    ppermute x13, waiting for transfers between devices, ring_gather(): pieces.append(lax.ppermute(block, 'pair', perm))  34.1 us
    ppermute x13, starting transfers between devices, ring_gather(): pieces.append(lax.ppermute(block, 'pair', perm))  16.3 us
    dot_general x1, matrix products, local(): jnp.einsum('pac,pab->pcb', margin, halfway, preferred_element_type=jnp.fl...  14.9 us
  transfers between devices with their start and end apart: 14, of which 8 were waited for; matrix products, arithmetic and copies ran while one was open for 3% of the time, Pallas kernels for 0%

profile of v1, /device:TPU:3, one launch (start us, length us, event | category | flops | bytes accessed | tf_op | source)
XLA Modules:
  0.0 552.6 jit_solution(10277231326709480183)
XLA Ops:
  0.0 0.8 collective-permute-start
  0.8 1.2 dynamic_slice.15
  2.7 1.6 gather_fusion
  4.3 1.1 constant_dynamic-slice_fusion
  6.0 3.9 convolution_convert_fusion
  10.0 4.8 subtract_divide_fusion
  14.7 14.9 %fusion.6 = bf16[128,128,128]{2,1,0:T(8,128)(2,1)} fusion(bf16[128,128,128]{2,0,1:T(8,128)(2,1)} %convolution_convert_fusion, bf16[128,64,128]{2,1,0:T(8,128)(2,1)} %collective-permute-done, bf16[128,64,128]{2,1,0:T(8,128)(2,1)} %param.8, pred[]{:T(512)S(6)} %eq.62), kind=kOutput, calls=%fused_computation.12 | convolution fusion | flops 1094713344 | bytes 12582913 | tf_op jit(solution)/shard_map/pac,pab->pcb/dot_general | solution.py:62
  29.7 1.8 dynamic-slice_convert_fusion
  31.5 1.8 fusion.22
  33.3 1.4 copy.17
  34.6 64.2 %all_to_all.10 = bf16[128,64,128]{2,1,0:T(8,128)(2,1)S(1)} all-to-all(bf16[128,64,128]{2,1,0:T(8,128)(2,1)S(1)} %copy.17), channel_id=1, replica_groups=mesh['pair'=128,'aux'=2] {'pair'}, dimensions={0} | all-to-all | bytes 4194304 | tf_op jit(solution)/shard_map/all_to_all | solution.py:79
  98.8 4.3 stack.60
  103.1 375.7 %all_to_all.11 = bf16[256,256,128]{2,1,0:T(8,128)(2,1)} all-to-all(bf16[256,256,128]{2,1,0:T(8,128)(2,1)S(1)} %stack.60), channel_id=1, replica_groups=mesh['pair'=128,'aux'=2] {'pair','aux'}, dimensions={0} | all-to-all | bytes 33554432 | tf_op jit(solution)/shard_map/all_to_all | solution.py:13
  478.7 11.0 %constant_dynamic-update-slice_fusion.7 = (bf16[8,64,128]{2,1,0:T(8,128)(2,1)S(1)}, bf16[64,128]{1,0:T(8,128)(2,1)S(1)}) fusion(bf16[128,512,128]{2,1,0:T(8,128)(2,1)} %bitcast.57, s32[]{:T(128)S(6)} %select_n.115, bf16[128,64,128]{2,1,0:T(8,128)(2,1)S(1)} %all_to_all.10), kind=kOutput, calls=%fused_computation.49 | convolution fusion | flops 1082179584 | bytes 19038212 | tf_op jit(solution)/shard_map/dot_general | solution.py:83
  490.3 4.1 collective-permute-start.5
  494.4 3.5 collective-permute-start.4
  498.2 1.0 collective-permute-start.2
  499.1 3.8 collective-permute-done.2
  503.0 2.0 collective-permute-start.7
  505.0 1.6 collective-permute-done.7
  506.6 1.6 collective-permute-start.10
  509.0 2.6 collective-permute-done.10
  511.6 2.1 collective-permute-done.9
  513.7 1.3 collective-permute-done.8
  515.1 1.1 collective-permute-start.12
  516.2 1.6 collective-permute-start.11
  517.8 7.2 %collective-permute-done.12 = bf16[4,8,64,128]{3,2,1,0:T(8,128)(2,1)S(1)} collective-permute-done((bf16[4,8,64,128]{3,2,1,0:T(8,128)(2,1)S(1)}, bf16[4,8,64,128]{3,2,1,0:T(8,128)(2,1)S(1)}, u32[]{:S(2)}, u32[]{:S(2)}) %collective-permute-start.12) | collective-permute-done | bytes 524320 | tf_op jit(solution)/shard_map/ppermute | solution.py:27
  525.0 13.4 %collective-permute-done.11 = bf16[4,8,64,128]{3,2,1,0:T(8,128)(2,1)S(1)} collective-permute-done((bf16[4,8,64,128]{3,2,1,0:T(8,128)(2,1)S(1)}, bf16[4,8,64,128]{3,2,1,0:T(8,128)(2,1)S(1)}, u32[]{:S(2)}, u32[]{:S(2)}) %collective-permute-start.11) | collective-permute-done | bytes 524320 | tf_op jit(solution)/shard_map/ppermute | solution.py:27
  538.4 2.0 collective-permute-done.13
  540.7 1.7 fusion.25
  542.6 1.3 copy-done.3
  543.9 8.7 %subtract_convert_fusion = bf16[128,64,128]{2,1,0:T(8,128)(2,1)} fusion(f32[128,64,128]{2,1,0:T(8,128)} %get-tuple-element.8, f32[128,64,128]{2,1,0:T(8,128)S(1)} %copy-done.3, bf16[128,128,128]{2,0,1:T(8,128)(2,1)S(1)} %copy-done.2, bf16[128,64,128]{2,0,1:T(8,128)(2,1)S(1)} %fusion.25), kind=kOutput, calls=%fused_computation.9 | convolution fusion | flops 271581184 | bytes 16777216 | tf_op jit(solution)/shard_map/pca,pba->pcb/dot_general | solution.py:101
  (42 shorter events, 3.4 us)
Async XLA Ops:
  0.0 6.0 %copy-start = (bf16[8,128,128]{2,1,0:T(8,128)(2,1)S(1)}, bf16[8,128,128]{2,1,0:T(8,128)(2,1)}, u32[]{:S(2)}) copy-start(bf16[8,128,128]{2,1,0:T(8,128)(2,1)} %param.10) | copy-start | bytes 786436
  0.0 10.0 %copy-start.6 = (f32[128,128]{1,0:T(8,128)S(1)}, f32[128,128]{1,0:T(8,128)}, u32[]{:S(2)}) copy-start(f32[128,128]{1,0:T(8,128)} %param.13) | copy-start | bytes 196612
  0.0 10.0 %copy-start.4 = (bf16[128,64,128]{2,1,0:T(8,128)(2,1)S(1)}, bf16[128,64,128]{2,1,0:T(8,128)(2,1)}, u32[]{:S(2)}) copy-start(bf16[128,64,128]{2,1,0:T(8,128)(2,1)} %param.9) | copy-start | bytes 6291460
  0.0 14.7 %collective-permute-start = (bf16[128,64,128]{2,1,0:T(8,128)(2,1)}, bf16[128,64,128]{2,1,0:T(8,128)(2,1)}, u32[]{:S(2)}, u32[]{:S(2)}) collective-permute-start(bf16[128,64,128]{2,1,0:T(8,128)(2,1)} %param.8), channel_id=1, source_target_pairs={{0,1},{1,0},{2,3},{3,2},{4,5},{5,4},{6,7},{7,6},{8,9},{9,8},{10,11... | collective-permute-start | bytes 6291464 | tf_op jit(solution)/shard_map/ppermute | solution.py:47
  4.3 5.7 %copy-start.5 = (bf16[128,64,128]{2,1,0:T(8,128)(2,1)S(1)}, bf16[128,64,128]{2,1,0:T(8,128)(2,1)}, u32[]{:S(2)}) copy-start(bf16[128,64,128]{2,1,0:T(8,128)(2,1)} %param.8) | copy-start | bytes 6291460
  29.7 1.8 copy-start.8
  33.2 65.6 %copy-start.7 = (bf16[1,256,128]{2,1,0:T(8,128)(2,1)S(1)}, bf16[1,256,128]{2,1,0:T(8,128)(2,1)}, u32[]{:S(2)}) copy-start(bf16[1,256,128]{2,1,0:T(8,128)(2,1)} %param.12) | copy-start | bytes 196612
  489.8 8.4 %collective-permute-start.1 = (bf16[64,128]{1,0:T(8,128)(2,1)S(1)}, bf16[64,128]{1,0:T(8,128)(2,1)S(1)}, u32[]{:S(2)}, u32[]{:S(2)}) collective-permute-start(bf16[64,128]{1,0:T(8,128)(2,1)S(1)} %get-tuple-element.16), channel_id=1, source_target_pairs={{0,8},{2,10},{4,12},{6,14},{8,16},{10,18},{12,20},{14,22},{16,24},... | collective-permute-start | bytes 49160 | tf_op jit(solution)/shard_map/ppermute | solution.py:27
  489.9 15.1 %collective-permute-start.6 = (bf16[64,128]{1,0:T(8,128)(2,1)S(1)}, bf16[64,128]{1,0:T(8,128)(2,1)S(1)}, u32[]{:S(2)}, u32[]{:S(2)}) collective-permute-start(bf16[64,128]{1,0:T(8,128)(2,1)S(1)} %get-tuple-element.16), channel_id=1, source_target_pairs={{0,48},{2,50},{4,52},{6,54},{8,56},{10,58},{12,60},{14,62},{16,0},... | collective-permute-start | bytes 49160 | tf_op jit(solution)/shard_map/ppermute | solution.py:27
  490.3 14.7 %collective-permute-start.5 = (bf16[64,128]{1,0:T(8,128)(2,1)S(1)}, bf16[64,128]{1,0:T(8,128)(2,1)S(1)}, u32[]{:S(2)}, u32[]{:S(2)}) collective-permute-start(bf16[64,128]{1,0:T(8,128)(2,1)S(1)} %get-tuple-element.16), channel_id=1, source_target_pairs={{0,40},{2,42},{4,44},{6,46},{8,48},{10,50},{12,52},{14,54},{16,56}... | collective-permute-start | bytes 49160 | tf_op jit(solution)/shard_map/ppermute | solution.py:27
  494.4 10.5 %collective-permute-start.4 = (bf16[64,128]{1,0:T(8,128)(2,1)S(1)}, bf16[64,128]{1,0:T(8,128)(2,1)S(1)}, u32[]{:S(2)}, u32[]{:S(2)}) collective-permute-start(bf16[64,128]{1,0:T(8,128)(2,1)S(1)} %get-tuple-element.16), channel_id=1, source_target_pairs={{0,32},{2,34},{4,36},{6,38},{8,40},{10,42},{12,44},{14,46},{16,48}... | collective-permute-start | bytes 49160 | tf_op jit(solution)/shard_map/ppermute | solution.py:27
  497.9 7.0 %collective-permute-start.3 = (bf16[64,128]{1,0:T(8,128)(2,1)S(1)}, bf16[64,128]{1,0:T(8,128)(2,1)S(1)}, u32[]{:S(2)}, u32[]{:S(2)}) collective-permute-start(bf16[64,128]{1,0:T(8,128)(2,1)S(1)} %get-tuple-element.16), channel_id=1, source_target_pairs={{0,24},{2,26},{4,28},{6,30},{8,32},{10,34},{12,36},{14,38},{16,40}... | collective-permute-start | bytes 49160 | tf_op jit(solution)/shard_map/ppermute | solution.py:27
  498.2 4.8 collective-permute-start.2
  503.0 3.7 collective-permute-start.7
  506.6 4.9 collective-permute-start.10
  508.2 5.4 collective-permute-start.9
  509.0 6.0 %collective-permute-start.8 = (bf16[8,64,128]{2,1,0:T(8,128)(2,1)S(1)}, bf16[8,64,128]{2,1,0:T(8,128)(2,1)S(1)}, u32[]{:S(2)}, u32[]{:S(2)}) collective-permute-start(bf16[8,64,128]{2,1,0:T(8,128)(2,1)S(1)} %constant_dynamic-update-slice_fusion), channel_id=1, source_target_pairs={{0,2},{2,4},{4,6},{6,0},{8,10},{10,12},{12,14},{14,8},{16,18},{18,... | collective-permute-start | bytes 393224 | tf_op jit(solution)/shard_map/ppermute | solution.py:27
  515.1 9.9 %collective-permute-start.12 = (bf16[4,8,64,128]{3,2,1,0:T(8,128)(2,1)S(1)}, bf16[4,8,64,128]{3,2,1,0:T(8,128)(2,1)S(1)}, u32[]{:S(2)}, u32[]{:S(2)}) collective-permute-start(bf16[4,8,64,128]{3,2,1,0:T(8,128)(2,1)S(1)} %get-tuple-element.12), channel_id=1, source_target_pairs={{0,128},{2,130},{4,132},{6,134},{8,136},{10,138},{12,140},{14,142}... | collective-permute-start | bytes 1572872 | tf_op jit(solution)/shard_map/ppermute | solution.py:27
  516.2 22.3 %collective-permute-start.11 = (bf16[4,8,64,128]{3,2,1,0:T(8,128)(2,1)S(1)}, bf16[4,8,64,128]{3,2,1,0:T(8,128)(2,1)S(1)}, u32[]{:S(2)}, u32[]{:S(2)}) collective-permute-start(bf16[4,8,64,128]{3,2,1,0:T(8,128)(2,1)S(1)} %get-tuple-element.12), channel_id=1, source_target_pairs={{0,64},{2,66},{4,68},{6,70},{8,72},{10,74},{12,76},{14,78},{16,80}... | collective-permute-start | bytes 1572872 | tf_op jit(solution)/shard_map/ppermute | solution.py:27
  517.7 22.7 %collective-permute-start.13 = (bf16[4,8,64,128]{3,2,1,0:T(8,128)(2,1)S(1)}, bf16[4,8,64,128]{3,2,1,0:T(8,128)(2,1)S(1)}, u32[]{:S(2)}, u32[]{:S(2)}) collective-permute-start(bf16[4,8,64,128]{3,2,1,0:T(8,128)(2,1)S(1)} %get-tuple-element.12), channel_id=1, source_target_pairs={{0,192},{2,194},{4,196},{6,198},{8,200},{10,202},{12,204},{14,206}... | collective-permute-start | bytes 1572872 | tf_op jit(solution)/shard_map/ppermute | solution.py:27
  540.4 2.2 copy-start.2
  540.4 3.5 copy-start.3
  543.9 8.7 %copy-start.1 = (bf16[8,128,128]{2,1,0:T(8,128)(2,1)S(1)}, bf16[8,128,128]{2,1,0:T(8,128)(2,1)}, u32[]{:S(2)}) copy-start(bf16[8,128,128]{2,1,0:T(8,128)(2,1)} %param.10) | copy-start | bytes 786436
